TPU v7x, 512 devices: a whole 4x8x8 slice. The times are simulated.
512 devices in a mesh: space: 64 (over z_hi, y, core), member: 8 (over z_lo, x).
Axes of the slice: x: 4, y: 8, z: 8 (z_hi: 4, z_lo: 2; z = z_hi * 2 + z_lo), core: 2. Of those that a mesh axis runs over, the one named last changes fastest.
Arguments:
- pressure: float32 [32, 10, 131072], P('member', None, 'space'), may hold values from -6 to 6
- heat: float32 [32, 10, 131072], P('member', None, 'space'), may hold values from -6 to 6
- log_cond: float32 [10, 131072], P(None, 'space'), may hold values from -1 to 1
- log_therm: float32 [10, 131072], P(None, 'space'), may hold values from -1 to 1
- frozen: float32 [10, 131072], P(None, 'space'), may hold values from 0 to 1
- frozen_flag: int32 [10, 131072], P(None, 'space'), may hold values 0 or 1
- recharge: float32 [32, 131072], P('member', 'space'), may hold values from -6 to 6
- face_cols: int32 [4, 16384], P(None, 'space'), may hold values from 0 to 2047
- face_weight: float32 [4, 16384], P(None, 'space'), may hold values from 0.05 to 0.3
- cot_pressure: float32 [32, 10, 131072], P('member', None, 'space'), may hold values from -6 to 6
- cot_heat: float32 [32, 10, 131072], P('member', None, 'space'), may hold values from -6 to 6
Outputs:
- new_pressure: float32 [32, 10, 131072], P('member', None, 'space')
- new_heat: float32 [32, 10, 131072], P('member', None, 'space')
- adj_pressure: float32 [32, 10, 131072], P('member', None, 'space')
- adj_heat: float32 [32, 10, 131072], P('member', None, 'space')
- param_grads: float32 [2, 10, 131072], P(None, None, ('space', 'member'))
All inputs are finite; a program needn't handle non-finite values. No bound on the sum of `frozen_flag` on one device may be relied on, other than what follows from the above.
Results may differ from a plain program's by a relative error of at most 0.00007.
Values sent between devices are 32-bit elements; how exact they have to be, the bound alone decides.
No kernel may reach another device: no remote copies, remote signals or barrier semaphores. Data moves between devices by JAX's collectives and lax.ppermute only.
A program may use at most 64 MiB of HBM per device.

v0:
```python
import jax
import jax.numpy as jnp
from jax import lax
from jax.sharding import PartitionSpec as P


def from_partner(value, axis, stride):
    mask = 2**stride
    pairs = [(source, source ^ mask) for source in range(lax.axis_size(axis))]
    return lax.ppermute(value, axis, pairs)


def spread(grad_iface):
    return jnp.pad(grad_iface, ((0, 0), (0, 1), (0, 0))) - jnp.pad(
        grad_iface, ((0, 0), (1, 0), (0, 0))
    )


def selector(columns, width):
    return (columns[:, None] == jnp.arange(width, dtype=jnp.int32)[None, :]).astype(jnp.float32)


def pick(values, select):
    return jnp.einsum("...c,kc->...k", values, select, precision=lax.Precision.HIGHEST)


def place(values, select):
    return jnp.einsum("...k,kc->...c", values, select, precision=lax.Precision.HIGHEST)


def body(
    pressure,
    heat,
    log_cond,
    log_therm,
    frozen,
    frozen_flag,
    recharge,
    face_cols,
    face_weight,
    cot_pressure,
    cot_heat,
):
    rounds = face_cols.shape[0]
    width = pressure.shape[2]
    blocked = frozen * frozen_flag.astype(jnp.float32)
    selects = [selector(face_cols[index], width) for index in range(rounds)]

    def advance(p_old, t_old, log_k, log_t, far_faces):
        cond = jnp.exp(log_k - 3.0 * blocked)
        therm = jnp.exp(log_t) * (1.0 + blocked)
        flow = 0.5 * (cond[:-1] + cond[1:]) * (p_old[:, 1:] - p_old[:, :-1])
        conduct = 0.5 * (therm[:-1] + therm[1:]) * (t_old[:, 1:] - t_old[:, :-1])
        carried = flow * 0.5 * (t_old[:, :-1] + t_old[:, 1:])
        p_rate = spread(flow)
        p_rate = p_rate.at[:, 0].add(recharge)
        t_rate = spread(conduct) + 0.5 * spread(carried)
        fields = jnp.stack([p_old, t_old])
        coeffs = jnp.stack([cond, therm])
        for index in range(rounds):
            select = selects[index]
            weight = face_weight[index]
            own = pick(fields, select)
            coef = pick(coeffs, select)
            update = weight * coef[:, None] * (far_faces[index] - own)
            added = place(update, select)
            p_rate = p_rate + added[0]
            t_rate = t_rate + added[1]
        return (p_old + 0.1 * p_rate, t_old + 0.1 * t_rate)

    fields_in = jnp.stack([pressure, heat])
    remotes = []
    for index in range(rounds):
        sending = pick(fields_in, selects[index])
        remotes.append(from_partner(sending, "space", index))
    remotes = jnp.stack(remotes)
    (new_pressure, new_heat), pullback = jax.vjp(
        advance, pressure, heat, log_cond, log_therm, remotes
    )
    adj_pressure, adj_heat, grad_k, grad_t, grad_far = pullback((cot_pressure, cot_heat))
    extra = None
    for index in range(rounds):
        coming = from_partner(grad_far[index], "space", index)
        term = place(coming, selects[index])
        extra = term if extra is None else extra + term
    adj_pressure = adj_pressure + extra[0]
    adj_heat = adj_heat + extra[1]
    grads = jnp.stack([grad_k, grad_t])
    summed = lax.psum(grads, "member")
    share = grads.shape[2] // lax.axis_size("member")
    owned = lax.dynamic_slice_in_dim(summed, lax.axis_index("member") * share, share, 2)
    return (new_pressure, new_heat, adj_pressure, adj_heat, owned)


def solution(mesh):
    placed = (
        P("member", None, "space"),
        P("member", None, "space"),
        P(None, "space"),
        P(None, "space"),
        P(None, "space"),
        P(None, "space"),
        P("member", "space"),
        P(None, "space"),
        P(None, "space"),
        P("member", None, "space"),
        P("member", None, "space"),
    )
    return jax.shard_map(
        body,
        mesh=mesh,
        in_specs=placed,
        out_specs=(
            P("member", None, "space"),
            P("member", None, "space"),
            P("member", None, "space"),
            P("member", None, "space"),
            P(None, None, ("space", "member")),
        ),
        check_vma=False,
    )
```

profile of v0, /device:TPU:8, one launch (start us, length us, event | category | flops | bytes accessed | tf_op | source)
XLA Modules:
  0.0 171.1 jit_solution(9766011143822614567)
XLA Ops:
  9.6 2.1 %fusion.26 = f32[2,4,10,256]{3,2,1,0:T(8,128)} fusion(s32[256]{0:T(256)S(1)} %bitcast.222, f32[1,4,10,2048]{3,2,1,0:T(8,128)S(1)} %get-tuple-element.51, f32[1,4,10,2048]{3,2,1,0:T(8,128)S(1)} %get-tuple-element.72), kind=kOutput, calls=%fused_computation.24 | convolution fusion | flops 504004608 | bytes 738304 | tf_op jit(solution)/shard_map/...c,kc->...k/dot_general | solution.py:24
  11.6 4.5 %collective-permute-start.2 = (f32[2,4,10,256]{3,2,1,0:T(8,128)}, f32[2,4,10,256]{3,2,1,0:T(8,128)}, u32[]{:S(2)}, u32[]{:S(2)}) collective-permute-start(f32[2,4,10,256]{3,2,1,0:T(8,128)} %fusion.26), channel_id=1, source_target_pairs={{0,32},{8,40},{16,48},{24,56},{32,0},{40,8},{48,16},{56,24},{64,96... | collective-permute-start | bytes 245768 | tf_op jit(solution)/shard_map/ppermute | solution.py:10
  16.1 2.1 %fusion.12 = f32[2,4,10,256]{3,2,1,0:T(8,128)} fusion(s32[256]{0:T(256)S(1)} %bitcast.229, f32[1,4,10,2048]{3,2,1,0:T(8,128)S(1)} %get-tuple-element.51, f32[1,4,10,2048]{3,2,1,0:T(8,128)S(1)} %get-tuple-element.72), kind=kOutput, calls=%fused_computation.16 | convolution fusion | flops 504004608 | bytes 738304 | tf_op jit(solution)/shard_map/...c,kc->...k/dot_general | solution.py:24
  18.2 5.0 %collective-permute-start.3 = (f32[2,4,10,256]{3,2,1,0:T(8,128)}, f32[2,4,10,256]{3,2,1,0:T(8,128)}, u32[]{:S(2)}, u32[]{:S(2)}) collective-permute-start(f32[2,4,10,256]{3,2,1,0:T(8,128)} %fusion.12), channel_id=1, source_target_pairs={{0,64},{8,72},{16,80},{24,88},{32,96},{40,104},{48,112},{56,120},{... | collective-permute-start | bytes 245768 | tf_op jit(solution)/shard_map/ppermute | solution.py:10
  23.2 2.1 %fusion.41 = f32[2,4,10,256]{3,2,1,0:T(8,128)} fusion(s32[256]{0:T(256)S(1)} %bitcast.215, f32[1,4,10,2048]{3,2,1,0:T(8,128)S(1)} %get-tuple-element.51, f32[1,4,10,2048]{3,2,1,0:T(8,128)S(1)} %get-tuple-element.72), kind=kOutput, calls=%fused_computation.33 | convolution fusion | flops 504004608 | bytes 738304 | tf_op jit(solution)/shard_map/...c,kc->...k/dot_general | solution.py:24
  25.3 3.4 %collective-permute-start.1 = (f32[2,4,10,256]{3,2,1,0:T(8,128)}, f32[2,4,10,256]{3,2,1,0:T(8,128)}, u32[]{:S(2)}, u32[]{:S(2)}) collective-permute-start(f32[2,4,10,256]{3,2,1,0:T(8,128)} %fusion.41), channel_id=1, source_target_pairs={{0,16},{8,24},{16,0},{24,8},{32,48},{40,56},{48,32},{56,40},{64,80... | collective-permute-start | bytes 245768 | tf_op jit(solution)/shard_map/ppermute | solution.py:10
  28.7 2.1 %fusion.54 = f32[2,4,10,256]{3,2,1,0:T(8,128)} fusion(s32[256]{0:T(256)S(1)} %bitcast.208, f32[1,4,10,2048]{3,2,1,0:T(8,128)S(1)} %get-tuple-element.51, f32[1,4,10,2048]{3,2,1,0:T(8,128)S(1)} %get-tuple-element.72), kind=kOutput, calls=%fused_computation.40 | convolution fusion | flops 504004608 | bytes 738304 | tf_op jit(solution)/shard_map/...c,kc->...k/dot_general | solution.py:24
  30.7 2.1 %collective-permute-start = (f32[2,4,10,256]{3,2,1,0:T(8,128)}, f32[2,4,10,256]{3,2,1,0:T(8,128)}, u32[]{:S(2)}, u32[]{:S(2)}) collective-permute-start(f32[2,4,10,256]{3,2,1,0:T(8,128)} %fusion.54), channel_id=1, source_target_pairs={{0,8},{8,0},{16,24},{24,16},{32,40},{40,32},{48,56},{56,48},{64,72... | collective-permute-start | bytes 245768 | tf_op jit(solution)/shard_map/ppermute | solution.py:10
  35.8 2.6 %multiply_reduce_fusion.4 = (f32[2,10,256]{2,1,0:T(8,128)S(1)}, f32[2,4,10,256]{3,2,1,0:T(8,128)S(1)}) fusion(f32[2,4,10,256]{3,2,1,0:T(8,128)} %collective-permute-done.2, f32[2,4,10,256]{3,2,1,0:T(8,128)} %fusion.26, s32[256]{0:T(256)S(1)} %bitcast.223, f32[1,4,10,2048]{3,2,1,0:T(8,128)} %get-tuple-element.74, f32[1,4,10,2048]{3,2,1,0:T(8,128)S(1)} %get-tuple-element.46), kind=kOutput, calls=%fused_computation.160 | convolution fusion | flops 504060928 | bytes 922624 | tf_op jit(solution)/shard_map/transpose(jvp(...k,kc->...c))/dot_general | solution.py:28
  39.3 2.4 %multiply_reduce_fusion.5 = (f32[2,10,256]{2,1,0:T(8,128)S(1)}, f32[2,4,10,256]{3,2,1,0:T(8,128)S(1)}) fusion(f32[2,4,10,256]{3,2,1,0:T(8,128)} %collective-permute-done.3, f32[2,4,10,256]{3,2,1,0:T(8,128)} %fusion.12, s32[256]{0:T(256)S(1)} %bitcast.230, f32[1,4,10,2048]{3,2,1,0:T(8,128)S(1)} %copy-done.11, f32[1,4,10,2048]{3,2,1,0:T(8,128)S(1)} %get-tuple-element.46), kind=kOutput, calls=%fused_computation.161 | convolution fusion | flops 504060928 | bytes 922624 | tf_op jit(solution)/shard_map/transpose(jvp(...k,kc->...c))/dot_general | solution.py:28
  42.6 2.4 %multiply_reduce_fusion.3 = (f32[2,10,256]{2,1,0:T(8,128)S(1)}, f32[2,4,10,256]{3,2,1,0:T(8,128)S(1)}) fusion(f32[2,4,10,256]{3,2,1,0:T(8,128)} %collective-permute-done.1, f32[2,4,10,256]{3,2,1,0:T(8,128)} %fusion.41, s32[256]{0:T(256)S(1)} %bitcast.216, f32[1,4,10,2048]{3,2,1,0:T(8,128)S(1)} %copy-done.11, f32[1,4,10,2048]{3,2,1,0:T(8,128)S(1)} %get-tuple-element.46), kind=kOutput, calls=%fused_computation.159 | convolution fusion | flops 504060928 | bytes 922624 | tf_op jit(solution)/shard_map/transpose(jvp(...k,kc->...c))/dot_general | solution.py:28
  46.0 2.4 %multiply_reduce_fusion.2 = (f32[2,10,256]{2,1,0:T(8,128)S(1)}, f32[2,4,10,256]{3,2,1,0:T(8,128)S(1)}) fusion(f32[2,4,10,256]{3,2,1,0:T(8,128)} %collective-permute-done, f32[2,4,10,256]{3,2,1,0:T(8,128)} %fusion.54, s32[256]{0:T(256)S(1)} %bitcast.209, f32[1,4,10,2048]{3,2,1,0:T(8,128)S(1)} %copy-done.11, f32[1,4,10,2048]{3,2,1,0:T(8,128)S(1)} %get-tuple-element.46), kind=kOutput, calls=%fused_computation.158 | convolution fusion | flops 504060928 | bytes 922624 | tf_op jit(solution)/shard_map/transpose(jvp(...k,kc->...c))/dot_general | solution.py:28
  60.9 4.2 %collective-permute-start.6 = (f32[2,4,10,256]{3,2,1,0:T(8,128)}, f32[2,4,10,256]{3,2,1,0:T(8,128)}, u32[]{:S(2)}, u32[]{:S(2)}) collective-permute-start(f32[2,4,10,256]{3,2,1,0:T(8,128)} %get-tuple-element.43), channel_id=1, source_target_pairs={{0,32},{8,40},{16,48},{24,56},{32,0},{40,8},{48,16},{56,24},{64,96... | collective-permute-start | bytes 245768 | tf_op jit(solution)/shard_map/ppermute | solution.py:10
  65.0 2.6 %collective-permute-start.5 = (f32[2,4,10,256]{3,2,1,0:T(8,128)}, f32[2,4,10,256]{3,2,1,0:T(8,128)}, u32[]{:S(2)}, u32[]{:S(2)}) collective-permute-start(f32[2,4,10,256]{3,2,1,0:T(8,128)} %get-tuple-element.44), channel_id=1, source_target_pairs={{0,16},{8,24},{16,0},{24,8},{32,48},{40,56},{48,32},{56,40},{64,80... | collective-permute-start | bytes 245768 | tf_op jit(solution)/shard_map/ppermute | solution.py:10
  67.6 6.7 %collective-permute-start.7 = (f32[2,4,10,256]{3,2,1,0:T(8,128)}, f32[2,4,10,256]{3,2,1,0:T(8,128)}, u32[]{:S(2)}, u32[]{:S(2)}) collective-permute-start(f32[2,4,10,256]{3,2,1,0:T(8,128)} %get-tuple-element.42), channel_id=1, source_target_pairs={{0,64},{8,72},{16,80},{24,88},{32,96},{40,104},{48,112},{56,120},{... | collective-permute-start | bytes 245768 | tf_op jit(solution)/shard_map/ppermute | solution.py:10
  74.4 1.9 %collective-permute-start.4 = (f32[2,4,10,256]{3,2,1,0:T(8,128)}, f32[2,4,10,256]{3,2,1,0:T(8,128)}, u32[]{:S(2)}, u32[]{:S(2)}) collective-permute-start(f32[2,4,10,256]{3,2,1,0:T(8,128)} %get-tuple-element.41), channel_id=1, source_target_pairs={{0,8},{8,0},{16,24},{24,16},{32,40},{40,32},{48,56},{56,48},{64,72... | collective-permute-start | bytes 245768 | tf_op jit(solution)/shard_map/ppermute | solution.py:10
  78.0 1.9 %fusion.52 = f32[2,4,10,2048]{3,2,1,0:T(8,128)S(1)} fusion(s32[256]{0:T(256)S(1)} %bitcast.213, f32[2,10,256]{2,1,0:T(8,128)S(1)} %copy-done.18, f32[2,4,10,256]{3,2,1,0:T(8,128)} %collective-permute-done, f32[2,4,10,256]{3,2,1,0:T(8,128)} %fusion.54), kind=kOutput, calls=%fused_computation.39 | convolution fusion | flops 503881728 | bytes 840704 | tf_op jit(solution)/shard_map/jvp(...k,kc->...c)/dot_general | solution.py:28
  79.9 1.9 %fusion.39 = f32[2,4,10,2048]{3,2,1,0:T(8,128)S(1)} fusion(s32[256]{0:T(256)S(1)} %bitcast.220, f32[2,10,256]{2,1,0:T(8,128)S(1)} %fusion.62, f32[2,4,10,256]{3,2,1,0:T(8,128)} %collective-permute-done.1, f32[2,4,10,256]{3,2,1,0:T(8,128)} %fusion.41), kind=kOutput, calls=%fused_computation.32 | convolution fusion | flops 503881728 | bytes 840704 | tf_op jit(solution)/shard_map/jvp(...k,kc->...c)/dot_general | solution.py:28
  81.9 2.0 %fusion.24 = f32[2,4,10,2048]{3,2,1,0:T(8,128)S(1)} fusion(s32[256]{0:T(256)S(1)} %bitcast.227, f32[2,10,256]{2,1,0:T(8,128)S(1)} %fusion.65, f32[2,4,10,256]{3,2,1,0:T(8,128)} %collective-permute-done.2, f32[2,4,10,256]{3,2,1,0:T(8,128)} %fusion.26), kind=kOutput, calls=%fused_computation.23 | convolution fusion | flops 503881728 | bytes 840704 | tf_op jit(solution)/shard_map/jvp(...k,kc->...c)/dot_general | solution.py:28
  83.9 1.9 %fusion.10 = f32[2,4,10,2048]{3,2,1,0:T(8,128)S(1)} fusion(s32[256]{0:T(256)S(1)} %bitcast.234, f32[2,10,256]{2,1,0:T(8,128)S(1)} %copy-done.20, f32[2,4,10,256]{3,2,1,0:T(8,128)} %collective-permute-done.3, f32[2,4,10,256]{3,2,1,0:T(8,128)} %fusion.12), kind=kOutput, calls=%fused_computation.15 | convolution fusion | flops 503881728 | bytes 840704 | tf_op jit(solution)/shard_map/jvp(...k,kc->...c)/dot_general | solution.py:28
  90.4 1.8 %fusion.34 = f32[2,4,10,2048]{3,2,1,0:T(8,128)S(1)} fusion(f32[2,4,10,256]{3,2,1,0:T(8,128)} %collective-permute-done.5, s32[256]{0:T(256)S(1)} %bitcast.221), kind=kOutput, calls=%fused_computation.30 | convolution fusion | flops 503840768 | bytes 738304 | tf_op jit(solution)/shard_map/...k,kc->...c/dot_general | solution.py:28
  92.2 1.8 %fusion.4 = f32[2,4,10,2048]{3,2,1,0:T(8,128)S(1)} fusion(f32[2,4,10,256]{3,2,1,0:T(8,128)} %collective-permute-done.7, s32[256]{0:T(256)S(1)} %bitcast.235), kind=kOutput, calls=%fused_computation.12 | convolution fusion | flops 503840768 | bytes 738304 | tf_op jit(solution)/shard_map/...k,kc->...c/dot_general | solution.py:28
  94.1 2.1 %fusion.1 = f32[2,4,10,2048]{3,2,1,0:T(8,128)S(1)} fusion(f32[2,4,10,2048]{3,2,1,0:T(8,128)S(1)} %fusion.4, f32[2,4,10,2048]{3,2,1,0:T(8,128)S(1)} %fusion.19, f32[2,4,10,2048]{3,2,1,0:T(8,128)S(1)} %fusion.34, f32[2,4,10,256]{3,2,1,0:T(8,128)} %collective-permute-done.4, s32[256]{0:T(256)S(1)} %bitcast.214), kind=kOutput, calls=%fused_computation.2 | convolution fusion | flops 504332288 | bytes 2704384 | tf_op jit(solution)/shard_map/...k,kc->...c/dot_general | solution.py:28
  99.0 63.8 %all-reduce.24.cloned.1.call-done = f32[2,10,2048]{2,1,0:T(8,128)} async-done(((f32[2,10,2048]{2,1,0:T(8,128)}), f32[2,10,2048]{2,1,0:T(8,128)}) %all-reduce.24.cloned.1.call-update) | async-done | bytes 163856 | tf_op jit(solution)/shard_map/psum | solution.py:89
  (108 shorter events, 30.6 us)
Async XLA Ops:
  7.2 155.7 %all-reduce.24.cloned.1.call-start = ((), (), s32[]{:S(2)}) async-start(), calls=%async_computation | async-start | bytes 524288 | tf_op jit(solution)/shard_map/psum | solution.py:89
  11.6 24.1 %collective-permute-start.2 = (f32[2,4,10,256]{3,2,1,0:T(8,128)}, f32[2,4,10,256]{3,2,1,0:T(8,128)}, u32[]{:S(2)}, u32[]{:S(2)}) collective-permute-start(f32[2,4,10,256]{3,2,1,0:T(8,128)} %fusion.26), channel_id=1, source_target_pairs={{0,32},{8,40},{16,48},{24,56},{32,0},{40,8},{48,16},{56,24},{64,96... | collective-permute-start | bytes 245768 | tf_op jit(solution)/shard_map/ppermute | solution.py:10
  18.2 21.1 %collective-permute-start.3 = (f32[2,4,10,256]{3,2,1,0:T(8,128)}, f32[2,4,10,256]{3,2,1,0:T(8,128)}, u32[]{:S(2)}, u32[]{:S(2)}) collective-permute-start(f32[2,4,10,256]{3,2,1,0:T(8,128)} %fusion.12), channel_id=1, source_target_pairs={{0,64},{8,72},{16,80},{24,88},{32,96},{40,104},{48,112},{56,120},{... | collective-permute-start | bytes 245768 | tf_op jit(solution)/shard_map/ppermute | solution.py:10
  25.3 7.6 %copy-start.12 = (f32[10,2048]{1,0:T(8,128)S(1)}, f32[10,2048]{1,0:T(8,128)}, u32[]{:S(2)}) copy-start(f32[10,2048]{1,0:T(8,128)} %param.16) | copy-start | bytes 245764
  25.3 7.6 %copy-start.13 = (f32[10,2048]{1,0:T(8,128)S(1)}, f32[10,2048]{1,0:T(8,128)}, u32[]{:S(2)}) copy-start(f32[10,2048]{1,0:T(8,128)} %param.17) | copy-start | bytes 245764
  25.3 7.6 %copy-start.15 = (s32[10,2048]{1,0:T(8,128)S(1)}, s32[10,2048]{1,0:T(8,128)}, u32[]{:S(2)}) copy-start(s32[10,2048]{1,0:T(8,128)} %param.18) | copy-start | bytes 245764
  25.3 17.3 %collective-permute-start.1 = (f32[2,4,10,256]{3,2,1,0:T(8,128)}, f32[2,4,10,256]{3,2,1,0:T(8,128)}, u32[]{:S(2)}, u32[]{:S(2)}) collective-permute-start(f32[2,4,10,256]{3,2,1,0:T(8,128)} %fusion.41), channel_id=1, source_target_pairs={{0,16},{8,24},{16,0},{24,8},{32,48},{40,56},{48,32},{56,40},{64,80... | collective-permute-start | bytes 245768 | tf_op jit(solution)/shard_map/ppermute | solution.py:10
  28.7 4.3 %copy-start.6 = (f32[4,10,2048]{2,0,1:T(4,128)S(1)}, f32[4,10,2048]{2,0,1:T(4,128)}, u32[]{:S(2)}) copy-start(f32[4,10,2048]{2,0,1:T(4,128)} %param.23) | copy-start | bytes 983044
  28.7 4.3 %copy-start.7 = (f32[4,10,2048]{2,0,1:T(4,128)S(1)}, f32[4,10,2048]{2,0,1:T(4,128)}, u32[]{:S(2)}) copy-start(f32[4,10,2048]{2,0,1:T(4,128)} %param.22) | copy-start | bytes 983044
  30.7 15.2 %collective-permute-start = (f32[2,4,10,256]{3,2,1,0:T(8,128)}, f32[2,4,10,256]{3,2,1,0:T(8,128)}, u32[]{:S(2)}, u32[]{:S(2)}) collective-permute-start(f32[2,4,10,256]{3,2,1,0:T(8,128)} %fusion.54), channel_id=1, source_target_pairs={{0,8},{8,0},{16,24},{24,16},{32,40},{40,32},{48,56},{56,48},{64,72... | collective-permute-start | bytes 245768 | tf_op jit(solution)/shard_map/ppermute | solution.py:10
  35.7 9.3 %copy-start.25 = (f32[1,256]{1,0:T(1,128)}, f32[1,256]{1,0:T(1,128)S(1)}, u32[]{:S(2)}) copy-start(f32[1,256]{1,0:T(1,128)S(1)} %get-tuple-element.57) | copy-start | bytes 3076
  35.7 12.7 %copy-start.23 = (f32[1,256]{1,0:T(1,128)}, f32[1,256]{1,0:T(1,128)S(1)}, u32[]{:S(2)}) copy-start(f32[1,256]{1,0:T(1,128)S(1)} %get-tuple-element.56) | copy-start | bytes 3076
  49.5 3.6 %copy-start.24 = (f32[1,256]{1,0:T(1,128)S(1)}, f32[1,256]{1,0:T(1,128)}, u32[]{:S(2)}) copy-start(f32[1,256]{1,0:T(1,128)} %copy-done.23) | copy-start | bytes 3076
  50.7 4.8 %copy-start.19 = (f32[2,10,256]{2,1,0:T(8,128)}, f32[2,10,256]{2,1,0:T(8,128)S(1)}, u32[]{:S(2)}) copy-start(f32[2,10,256]{2,1,0:T(8,128)S(1)} %fusion.68) | copy-start | bytes 61444
  54.3 4.7 %copy-start.17 = (f32[2,10,256]{2,1,0:T(8,128)}, f32[2,10,256]{2,1,0:T(8,128)S(1)}, u32[]{:S(2)}) copy-start(f32[2,10,256]{2,1,0:T(8,128)S(1)} %fusion.59) | copy-start | bytes 61444
  60.9 17.1 %copy-start.18 = (f32[2,10,256]{2,1,0:T(8,128)S(1)}, f32[2,10,256]{2,1,0:T(8,128)}, u32[]{:S(2)}) copy-start(f32[2,10,256]{2,1,0:T(8,128)} %copy-done.17) | copy-start | bytes 61444
  60.9 27.7 %collective-permute-start.6 = (f32[2,4,10,256]{3,2,1,0:T(8,128)}, f32[2,4,10,256]{3,2,1,0:T(8,128)}, u32[]{:S(2)}, u32[]{:S(2)}) collective-permute-start(f32[2,4,10,256]{3,2,1,0:T(8,128)} %get-tuple-element.43), channel_id=1, source_target_pairs={{0,32},{8,40},{16,48},{24,56},{32,0},{40,8},{48,16},{56,24},{64,96... | collective-permute-start | bytes 245768 | tf_op jit(solution)/shard_map/ppermute | solution.py:10
  65.0 25.3 %collective-permute-start.5 = (f32[2,4,10,256]{3,2,1,0:T(8,128)}, f32[2,4,10,256]{3,2,1,0:T(8,128)}, u32[]{:S(2)}, u32[]{:S(2)}) collective-permute-start(f32[2,4,10,256]{3,2,1,0:T(8,128)} %get-tuple-element.44), channel_id=1, source_target_pairs={{0,16},{8,24},{16,0},{24,8},{32,48},{40,56},{48,32},{56,40},{64,80... | collective-permute-start | bytes 245768 | tf_op jit(solution)/shard_map/ppermute | solution.py:10
  67.6 24.6 %collective-permute-start.7 = (f32[2,4,10,256]{3,2,1,0:T(8,128)}, f32[2,4,10,256]{3,2,1,0:T(8,128)}, u32[]{:S(2)}, u32[]{:S(2)}) collective-permute-start(f32[2,4,10,256]{3,2,1,0:T(8,128)} %get-tuple-element.42), channel_id=1, source_target_pairs={{0,64},{8,72},{16,80},{24,88},{32,96},{40,104},{48,112},{56,120},{... | collective-permute-start | bytes 245768 | tf_op jit(solution)/shard_map/ppermute | solution.py:10
  74.4 19.7 %collective-permute-start.4 = (f32[2,4,10,256]{3,2,1,0:T(8,128)}, f32[2,4,10,256]{3,2,1,0:T(8,128)}, u32[]{:S(2)}, u32[]{:S(2)}) collective-permute-start(f32[2,4,10,256]{3,2,1,0:T(8,128)} %get-tuple-element.41), channel_id=1, source_target_pairs={{0,8},{8,0},{16,24},{24,16},{32,40},{40,32},{48,56},{56,48},{64,72... | collective-permute-start | bytes 245768 | tf_op jit(solution)/shard_map/ppermute | solution.py:10
  79.9 4.0 %copy-start.20 = (f32[2,10,256]{2,1,0:T(8,128)S(1)}, f32[2,10,256]{2,1,0:T(8,128)}, u32[]{:S(2)}) copy-start(f32[2,10,256]{2,1,0:T(8,128)} %copy-done.19) | copy-start | bytes 61444
  81.9 4.0 %copy-start = (f32[4,9,2048]{2,1,0:T(8,128)S(1)}, f32[4,9,2048]{2,1,0:T(8,128)}, u32[]{:S(2)}) copy-start(f32[4,9,2048]{2,1,0:T(8,128)} %get-tuple-element.38) | copy-start | bytes 884740
  81.9 4.0 %copy-start.9 = (f32[4,10,2048]{2,0,1:T(4,128)S(1)}, f32[4,10,2048]{2,0,1:T(4,128)}, u32[]{:S(2)}) copy-start(f32[4,10,2048]{2,0,1:T(4,128)} %param.14) | copy-start | bytes 983044
  81.9 4.0 %copy-start.10 = (f32[4,10,2048]{2,0,1:T(4,128)S(1)}, f32[4,10,2048]{2,0,1:T(4,128)}, u32[]{:S(2)}) copy-start(f32[4,10,2048]{2,0,1:T(4,128)} %param.13) | copy-start | bytes 983044
  (12 other events, 30.8 us)
Sparse Core Ops, SparseCore 0:
  77.2 85.6 all-reduce.23
where the time goes:
time: 172 us; the launch traced here: 171 us
  waiting for transfers between devices  63.9 us (37%)
  matrix products  45.5 us (26%)
  starting transfers between devices  30.4 us (18%)
  between operations  14.8 us (9%)
  local copies, waits for them, and re-layouts  8.84 us (5%)
  other arithmetic  7.6 us (4%)
    psum x1, waiting for transfers between devices, body(): summed = lax.psum(grads, 'member')  63.8 us
    ppermute x8, starting transfers between devices, from_partner(): return lax.ppermute(value, axis, pairs)  30.4 us
    dot_general x12, matrix products, place(): jnp.einsum('...k,kc->...c', values, select, precision=lax.Precision.HIGHEST)  25 us
    dot_general x16, matrix products, pick(): jnp.einsum('...c,kc->...k', values, select, precision=lax.Precision.HIGHEST)  20.4 us
    unnamed x60, local copies, waits for them, and re-layouts  6.25 us
  transfers between devices with their start and end apart: 9, of which 1 were waited for; matrix products, arithmetic and copies ran while one was open for 24% of the time, Pallas kernels for 0%

commit v1 on v0

--- a/solution.py
+++ b/solution.py
@@ -86,7 +86,7 @@
     adj_pressure = adj_pressure + extra[0]
     adj_heat = adj_heat + extra[1]
     grads = jnp.stack([grad_k, grad_t])
-    summed = lax.psum(grads, "member")
+    summed = jnp.sum(lax.all_gather(grads, "member"), axis=0)
     share = grads.shape[2] // lax.axis_size("member")
     owned = lax.dynamic_slice_in_dim(summed, lax.axis_index("member") * share, share, 2)
     return (new_pressure, new_heat, adj_pressure, adj_heat, owned)

time: 172 us -> 138 us (0.80)
  waiting for transfers between devices: 63.9 us -> 20.9 us
  other arithmetic: 7.6 us -> 14.1 us
  matrix products: 45.5 us -> 48.8 us
    psum x1 -> x0, waiting for transfers between devices: 63.8 us -> none  [body(): summed = lax.psum(grads, 'member')]
    all_gather x0 -> x1, waiting for transfers between devices: none -> 20.9 us  [body(): summed = jnp.sum(lax.all_gather(grads, 'member'), axis=0)]
    dot_general x12, matrix products: 25 us -> 28.1 us  [place(): jnp.einsum('...k,kc->...c', values, select, precision=lax.Precision.HIGHEST)]
    add x1, other arithmetic: 0.81 us -> 3.87 us  [advance(): return (p_old + 0.1 * p_rate, t_old + 0.1 * t_rate)]
    reduce_sum x0 -> x1, other arithmetic: none -> 1.76 us  [body(): summed = jnp.sum(lax.all_gather(grads, 'member'), axis=0)]
    unnamed x60 -> x54, local copies, waits for them, and re-layouts: 6.25 us -> 6.02 us
  transfers between devices with their start and end apart: 9 -> 9, of which waited for: 1 -> 1; matrix products, arithmetic and copies ran while one was open for 24% -> 36% of each run, Pallas kernels for 0% -> 0%
where the time goes in v1:
time: 138 us; the launch traced here: 137 us
  matrix products  48.8 us (35%)
  starting transfers between devices  30.3 us (22%)
  waiting for transfers between devices  20.9 us (15%)
  between operations  14.7 us (11%)
  other arithmetic  14.1 us (10%)
  local copies, waits for them, and re-layouts  8.09 us (6%)
    ppermute x8, starting transfers between devices, from_partner(): return lax.ppermute(value, axis, pairs)  30.2 us
    dot_general x12, matrix products, place(): jnp.einsum('...k,kc->...c', values, select, precision=lax.Precision.HIGHEST)  28.1 us
    all_gather x1, waiting for transfers between devices, body(): summed = jnp.sum(lax.all_gather(grads, 'member'), axis=0)  20.9 us
    dot_general x16, matrix products, pick(): jnp.einsum('...c,kc->...k', values, select, precision=lax.Precision.HIGHEST)  20.6 us
    unnamed x54, local copies, waits for them, and re-layouts  6.02 us
    add x1, other arithmetic, advance(): return (p_old + 0.1 * p_rate, t_old + 0.1 * t_rate)  3.87 us
  transfers between devices with their start and end apart: 9, of which 1 were waited for; matrix products, arithmetic and copies ran while one was open for 36% of the time, Pallas kernels for 0%

profile of v1, /device:TPU:8, one launch (start us, length us, event | category | flops | bytes accessed | tf_op | source)
XLA Modules:
  0.0 136.9 jit_solution(16743465916805671598)
XLA Ops:
  9.6 2.1 %fusion.26 = f32[2,4,10,256]{3,2,1,0:T(8,128)} fusion(s32[256]{0:T(256)S(1)} %bitcast.224, f32[1,4,10,2048]{3,2,1,0:T(8,128)S(1)} %get-tuple-element.56, f32[1,4,10,2048]{3,2,1,0:T(8,128)S(1)} %get-tuple-element.77), kind=kOutput, calls=%fused_computation.24 | convolution fusion | flops 504004608 | bytes 738304 | tf_op jit(solution)/shard_map/...c,kc->...k/dot_general | solution.py:24
  11.6 4.5 %collective-permute-start.2 = (f32[2,4,10,256]{3,2,1,0:T(8,128)}, f32[2,4,10,256]{3,2,1,0:T(8,128)}, u32[]{:S(2)}, u32[]{:S(2)}) collective-permute-start(f32[2,4,10,256]{3,2,1,0:T(8,128)} %fusion.26), channel_id=1, source_target_pairs={{0,32},{8,40},{16,48},{24,56},{32,0},{40,8},{48,16},{56,24},{64,96... | collective-permute-start | bytes 245768 | tf_op jit(solution)/shard_map/ppermute | solution.py:10
  16.1 2.1 %fusion.12 = f32[2,4,10,256]{3,2,1,0:T(8,128)} fusion(s32[256]{0:T(256)S(1)} %bitcast.231, f32[1,4,10,2048]{3,2,1,0:T(8,128)S(1)} %get-tuple-element.56, f32[1,4,10,2048]{3,2,1,0:T(8,128)S(1)} %get-tuple-element.77), kind=kOutput, calls=%fused_computation.16 | convolution fusion | flops 504004608 | bytes 738304 | tf_op jit(solution)/shard_map/...c,kc->...k/dot_general | solution.py:24
  18.2 5.2 %collective-permute-start.3 = (f32[2,4,10,256]{3,2,1,0:T(8,128)}, f32[2,4,10,256]{3,2,1,0:T(8,128)}, u32[]{:S(2)}, u32[]{:S(2)}) collective-permute-start(f32[2,4,10,256]{3,2,1,0:T(8,128)} %fusion.12), channel_id=1, source_target_pairs={{0,64},{8,72},{16,80},{24,88},{32,96},{40,104},{48,112},{56,120},{... | collective-permute-start | bytes 245768 | tf_op jit(solution)/shard_map/ppermute | solution.py:10
  23.4 2.1 %fusion.41 = f32[2,4,10,256]{3,2,1,0:T(8,128)} fusion(s32[256]{0:T(256)S(1)} %bitcast.217, f32[1,4,10,2048]{3,2,1,0:T(8,128)S(1)} %get-tuple-element.56, f32[1,4,10,2048]{3,2,1,0:T(8,128)S(1)} %get-tuple-element.77), kind=kOutput, calls=%fused_computation.33 | convolution fusion | flops 504004608 | bytes 738304 | tf_op jit(solution)/shard_map/...c,kc->...k/dot_general | solution.py:24
  25.4 3.2 %collective-permute-start.1 = (f32[2,4,10,256]{3,2,1,0:T(8,128)}, f32[2,4,10,256]{3,2,1,0:T(8,128)}, u32[]{:S(2)}, u32[]{:S(2)}) collective-permute-start(f32[2,4,10,256]{3,2,1,0:T(8,128)} %fusion.41), channel_id=1, source_target_pairs={{0,16},{8,24},{16,0},{24,8},{32,48},{40,56},{48,32},{56,40},{64,80... | collective-permute-start | bytes 245768 | tf_op jit(solution)/shard_map/ppermute | solution.py:10
  28.7 2.0 %fusion.54 = f32[2,4,10,256]{3,2,1,0:T(8,128)} fusion(s32[256]{0:T(256)S(1)} %bitcast.210, f32[1,4,10,2048]{3,2,1,0:T(8,128)S(1)} %get-tuple-element.56, f32[1,4,10,2048]{3,2,1,0:T(8,128)S(1)} %get-tuple-element.77), kind=kOutput, calls=%fused_computation.40 | convolution fusion | flops 504004608 | bytes 738304 | tf_op jit(solution)/shard_map/...c,kc->...k/dot_general | solution.py:24
  30.7 2.1 %collective-permute-start = (f32[2,4,10,256]{3,2,1,0:T(8,128)}, f32[2,4,10,256]{3,2,1,0:T(8,128)}, u32[]{:S(2)}, u32[]{:S(2)}) collective-permute-start(f32[2,4,10,256]{3,2,1,0:T(8,128)} %fusion.54), channel_id=1, source_target_pairs={{0,8},{8,0},{16,24},{24,16},{32,40},{40,32},{48,56},{56,48},{64,72... | collective-permute-start | bytes 245768 | tf_op jit(solution)/shard_map/ppermute | solution.py:10
  37.3 2.7 %multiply_reduce_fusion.4 = (f32[2,10,256]{2,1,0:T(8,128)S(1)}, f32[2,4,10,256]{3,2,1,0:T(8,128)S(1)}) fusion(f32[2,4,10,256]{3,2,1,0:T(8,128)} %collective-permute-done.2, f32[2,4,10,256]{3,2,1,0:T(8,128)} %fusion.26, s32[256]{0:T(256)S(1)} %bitcast.225, f32[1,4,10,2048]{3,2,1,0:T(8,128)} %get-tuple-element.79, f32[1,4,10,2048]{3,2,1,0:T(8,128)} %get-tuple-element.51), kind=kOutput, calls=%fused_computation.160 | convolution fusion | flops 504060928 | bytes 922624 | tf_op jit(solution)/shard_map/transpose(jvp(...k,kc->...c))/dot_general | solution.py:28
  40.9 2.4 %multiply_reduce_fusion.5 = (f32[2,10,256]{2,1,0:T(8,128)S(1)}, f32[2,4,10,256]{3,2,1,0:T(8,128)S(1)}) fusion(f32[2,4,10,256]{3,2,1,0:T(8,128)} %collective-permute-done.3, f32[2,4,10,256]{3,2,1,0:T(8,128)} %fusion.12, s32[256]{0:T(256)S(1)} %bitcast.232, f32[1,4,10,2048]{3,2,1,0:T(8,128)S(1)} %copy-done.9, f32[1,4,10,2048]{3,2,1,0:T(8,128)S(1)} %copy-done.8), kind=kOutput, calls=%fused_computation.161 | convolution fusion | flops 504060928 | bytes 922624 | tf_op jit(solution)/shard_map/transpose(jvp(...k,kc->...c))/dot_general | solution.py:28
  44.3 2.5 %multiply_reduce_fusion.3 = (f32[2,10,256]{2,1,0:T(8,128)S(1)}, f32[2,4,10,256]{3,2,1,0:T(8,128)S(1)}) fusion(f32[2,4,10,256]{3,2,1,0:T(8,128)} %collective-permute-done.1, f32[2,4,10,256]{3,2,1,0:T(8,128)} %fusion.41, s32[256]{0:T(256)S(1)} %bitcast.218, f32[1,4,10,2048]{3,2,1,0:T(8,128)S(1)} %copy-done.9, f32[1,4,10,2048]{3,2,1,0:T(8,128)S(1)} %copy-done.8), kind=kOutput, calls=%fused_computation.159 | convolution fusion | flops 504060928 | bytes 922624 | tf_op jit(solution)/shard_map/transpose(jvp(...k,kc->...c))/dot_general | solution.py:28
  47.7 2.4 %multiply_reduce_fusion.2 = (f32[2,10,256]{2,1,0:T(8,128)S(1)}, f32[2,4,10,256]{3,2,1,0:T(8,128)S(1)}) fusion(f32[2,4,10,256]{3,2,1,0:T(8,128)} %collective-permute-done, f32[2,4,10,256]{3,2,1,0:T(8,128)} %fusion.54, s32[256]{0:T(256)S(1)} %bitcast.211, f32[1,4,10,2048]{3,2,1,0:T(8,128)S(1)} %copy-done.9, f32[1,4,10,2048]{3,2,1,0:T(8,128)S(1)} %copy-done.8), kind=kOutput, calls=%fused_computation.158 | convolution fusion | flops 504060928 | bytes 922624 | tf_op jit(solution)/shard_map/transpose(jvp(...k,kc->...c))/dot_general | solution.py:28
  63.4 4.0 %collective-permute-start.6 = (f32[2,4,10,256]{3,2,1,0:T(8,128)}, f32[2,4,10,256]{3,2,1,0:T(8,128)}, u32[]{:S(2)}, u32[]{:S(2)}) collective-permute-start(f32[2,4,10,256]{3,2,1,0:T(8,128)} %get-tuple-element.48), channel_id=1, source_target_pairs={{0,32},{8,40},{16,48},{24,56},{32,0},{40,8},{48,16},{56,24},{64,96... | collective-permute-start | bytes 245768 | tf_op jit(solution)/shard_map/ppermute | solution.py:10
  67.4 2.6 %collective-permute-start.5 = (f32[2,4,10,256]{3,2,1,0:T(8,128)}, f32[2,4,10,256]{3,2,1,0:T(8,128)}, u32[]{:S(2)}, u32[]{:S(2)}) collective-permute-start(f32[2,4,10,256]{3,2,1,0:T(8,128)} %get-tuple-element.49), channel_id=1, source_target_pairs={{0,16},{8,24},{16,0},{24,8},{32,48},{40,56},{48,32},{56,40},{64,80... | collective-permute-start | bytes 245768 | tf_op jit(solution)/shard_map/ppermute | solution.py:10
  70.0 6.7 %collective-permute-start.7 = (f32[2,4,10,256]{3,2,1,0:T(8,128)}, f32[2,4,10,256]{3,2,1,0:T(8,128)}, u32[]{:S(2)}, u32[]{:S(2)}) collective-permute-start(f32[2,4,10,256]{3,2,1,0:T(8,128)} %get-tuple-element.47), channel_id=1, source_target_pairs={{0,64},{8,72},{16,80},{24,88},{32,96},{40,104},{48,112},{56,120},{... | collective-permute-start | bytes 245768 | tf_op jit(solution)/shard_map/ppermute | solution.py:10
  76.7 1.9 %collective-permute-start.4 = (f32[2,4,10,256]{3,2,1,0:T(8,128)}, f32[2,4,10,256]{3,2,1,0:T(8,128)}, u32[]{:S(2)}, u32[]{:S(2)}) collective-permute-start(f32[2,4,10,256]{3,2,1,0:T(8,128)} %get-tuple-element.46), channel_id=1, source_target_pairs={{0,8},{8,0},{16,24},{24,16},{32,40},{40,32},{48,56},{56,48},{64,72... | collective-permute-start | bytes 245768 | tf_op jit(solution)/shard_map/ppermute | solution.py:10
  79.4 1.9 %fusion.52 = f32[2,4,10,2048]{3,2,1,0:T(8,128)S(1)} fusion(s32[256]{0:T(256)S(1)} %bitcast.215, f32[2,10,256]{2,1,0:T(8,128)} %copy-done.18, f32[2,4,10,256]{3,2,1,0:T(8,128)} %collective-permute-done, f32[2,4,10,256]{3,2,1,0:T(8,128)} %fusion.54), kind=kOutput, calls=%fused_computation.39 | convolution fusion | flops 503881728 | bytes 840704 | tf_op jit(solution)/shard_map/jvp(...k,kc->...c)/dot_general | solution.py:28
  81.4 2.9 %fusion.39 = f32[2,4,10,2048]{3,2,1,0:T(8,128)} fusion(s32[256]{0:T(256)S(1)} %bitcast.222, f32[2,10,256]{2,1,0:T(8,128)S(1)} %fusion.62, f32[2,4,10,256]{3,2,1,0:T(8,128)} %collective-permute-done.1, f32[2,4,10,256]{3,2,1,0:T(8,128)} %fusion.41), kind=kOutput, calls=%fused_computation.32 | convolution fusion | flops 503881728 | bytes 840704 | tf_op jit(solution)/shard_map/jvp(...k,kc->...c)/dot_general | solution.py:28
  84.3 2.9 %fusion.24 = f32[2,4,10,2048]{3,2,1,0:T(8,128)} fusion(s32[256]{0:T(256)S(1)} %bitcast.229, f32[2,10,256]{2,1,0:T(8,128)S(1)} %fusion.65, f32[2,4,10,256]{3,2,1,0:T(8,128)} %collective-permute-done.2, f32[2,4,10,256]{3,2,1,0:T(8,128)} %fusion.26), kind=kOutput, calls=%fused_computation.23 | convolution fusion | flops 503881728 | bytes 840704 | tf_op jit(solution)/shard_map/jvp(...k,kc->...c)/dot_general | solution.py:28
  87.1 2.9 %fusion.10 = f32[2,4,10,2048]{3,2,1,0:T(8,128)} fusion(s32[256]{0:T(256)S(1)} %bitcast.236, f32[2,10,256]{2,1,0:T(8,128)S(1)} %copy-done.20, f32[2,4,10,256]{3,2,1,0:T(8,128)} %collective-permute-done.3, f32[2,4,10,256]{3,2,1,0:T(8,128)} %fusion.12), kind=kOutput, calls=%fused_computation.15 | convolution fusion | flops 503881728 | bytes 840704 | tf_op jit(solution)/shard_map/jvp(...k,kc->...c)/dot_general | solution.py:28
  90.5 3.9 %fusion.110 = (f32[4,10,2048]{2,1,0:T(8,128)S(1)}, f32[4,10,2048]{2,1,0:T(8,128)S(1)}) fusion(f32[2,4,10,2048]{3,2,1,0:T(8,128)} %fusion.10, f32[2,4,10,2048]{3,2,1,0:T(8,128)} %fusion.24, f32[2,4,10,2048]{3,2,1,0:T(8,128)} %fusion.39, f32[2,4,10,2048]{3,2,1,0:T(8,128)S(1)} %fusion.52, f32[4,9,2048]{2,1,0:T(8,128)} %multiply_multiply_fusion.1, ...), kind=kLoop, calls=%fused_computation.103 | loop fusion | flops 1310720 | bytes 4849664 | tf_op jit(solution)/shard_map/jvp()/add | solution.py:69
  99.9 1.8 %fusion.4 = f32[2,4,10,2048]{3,2,1,0:T(8,128)S(1)} fusion(f32[2,4,10,256]{3,2,1,0:T(8,128)} %collective-permute-done.7, s32[256]{0:T(256)S(1)} %bitcast.237), kind=kOutput, calls=%fused_computation.12 | convolution fusion | flops 503840768 | bytes 738304 | tf_op jit(solution)/shard_map/...k,kc->...c/dot_general | solution.py:28
  101.9 2.1 %fusion.1 = f32[2,4,10,2048]{3,2,1,0:T(8,128)S(1)} fusion(f32[2,4,10,2048]{3,2,1,0:T(8,128)S(1)} %fusion.4, f32[2,4,10,2048]{3,2,1,0:T(8,128)S(1)} %fusion.19, f32[2,4,10,2048]{3,2,1,0:T(8,128)S(1)} %fusion.34, f32[2,4,10,256]{3,2,1,0:T(8,128)} %collective-permute-done.4, s32[256]{0:T(256)S(1)} %bitcast.216), kind=kOutput, calls=%fused_computation.2 | convolution fusion | flops 504332288 | bytes 2704384 | tf_op jit(solution)/shard_map/...k,kc->...c/dot_general | solution.py:28
  106.7 20.9 %all-gather.3.cloned.1.call-done = f32[16,10,2048]{2,1,0:T(8,128)} async-done(((f32[2,10,2048]{2,1,0:T(8,128)}), f32[16,10,2048]{2,1,0:T(8,128)}) %all-gather.3.cloned.1.call-update) | async-done | bytes 1310736 | tf_op jit(solution)/shard_map/all_gather | solution.py:89
  (103 shorter events, 34.5 us)
Async XLA Ops:
  7.2 120.5 %all-gather.3.cloned.1.call-start = ((), (), s32[]{:S(2)}) async-start(), calls=%async_computation | async-start | bytes 2359296 | tf_op jit(solution)/shard_map/all_gather | solution.py:89
  11.6 25.6 %collective-permute-start.2 = (f32[2,4,10,256]{3,2,1,0:T(8,128)}, f32[2,4,10,256]{3,2,1,0:T(8,128)}, u32[]{:S(2)}, u32[]{:S(2)}) collective-permute-start(f32[2,4,10,256]{3,2,1,0:T(8,128)} %fusion.26), channel_id=1, source_target_pairs={{0,32},{8,40},{16,48},{24,56},{32,0},{40,8},{48,16},{56,24},{64,96... | collective-permute-start | bytes 245768 | tf_op jit(solution)/shard_map/ppermute | solution.py:10
  18.2 14.7 %copy-start.12 = (f32[10,2048]{1,0:T(8,128)S(1)}, f32[10,2048]{1,0:T(8,128)}, u32[]{:S(2)}) copy-start(f32[10,2048]{1,0:T(8,128)} %param.16) | copy-start | bytes 245764
  18.2 14.7 %copy-start.14 = (f32[10,2048]{1,0:T(8,128)S(1)}, f32[10,2048]{1,0:T(8,128)}, u32[]{:S(2)}) copy-start(f32[10,2048]{1,0:T(8,128)} %param.17) | copy-start | bytes 245764
  18.2 14.7 %copy-start.16 = (s32[10,2048]{1,0:T(8,128)S(1)}, s32[10,2048]{1,0:T(8,128)}, u32[]{:S(2)}) copy-start(s32[10,2048]{1,0:T(8,128)} %param.18) | copy-start | bytes 245764
  18.2 22.7 %collective-permute-start.3 = (f32[2,4,10,256]{3,2,1,0:T(8,128)}, f32[2,4,10,256]{3,2,1,0:T(8,128)}, u32[]{:S(2)}, u32[]{:S(2)}) collective-permute-start(f32[2,4,10,256]{3,2,1,0:T(8,128)} %fusion.12), channel_id=1, source_target_pairs={{0,64},{8,72},{16,80},{24,88},{32,96},{40,104},{48,112},{56,120},{... | collective-permute-start | bytes 245768 | tf_op jit(solution)/shard_map/ppermute | solution.py:10
  23.4 9.6 %copy-start.5 = (f32[4,10,2048]{2,0,1:T(4,128)S(1)}, f32[4,10,2048]{2,0,1:T(4,128)}, u32[]{:S(2)}) copy-start(f32[4,10,2048]{2,0,1:T(4,128)} %param.23) | copy-start | bytes 983044
  23.4 9.6 %copy-start.6 = (f32[4,10,2048]{2,0,1:T(4,128)S(1)}, f32[4,10,2048]{2,0,1:T(4,128)}, u32[]{:S(2)}) copy-start(f32[4,10,2048]{2,0,1:T(4,128)} %param.22) | copy-start | bytes 983044
  25.4 18.8 %collective-permute-start.1 = (f32[2,4,10,256]{3,2,1,0:T(8,128)}, f32[2,4,10,256]{3,2,1,0:T(8,128)}, u32[]{:S(2)}, u32[]{:S(2)}) collective-permute-start(f32[2,4,10,256]{3,2,1,0:T(8,128)} %fusion.41), channel_id=1, source_target_pairs={{0,16},{8,24},{16,0},{24,8},{32,48},{40,56},{48,32},{56,40},{64,80... | collective-permute-start | bytes 245768 | tf_op jit(solution)/shard_map/ppermute | solution.py:10
  30.7 17.0 %collective-permute-start = (f32[2,4,10,256]{3,2,1,0:T(8,128)}, f32[2,4,10,256]{3,2,1,0:T(8,128)}, u32[]{:S(2)}, u32[]{:S(2)}) collective-permute-start(f32[2,4,10,256]{3,2,1,0:T(8,128)} %fusion.54), channel_id=1, source_target_pairs={{0,8},{8,0},{16,24},{24,16},{32,40},{40,32},{48,56},{56,48},{64,72... | collective-permute-start | bytes 245768 | tf_op jit(solution)/shard_map/ppermute | solution.py:10
  35.9 5.0 %copy-start.8 = (f32[1,4,10,2048]{3,2,1,0:T(8,128)S(1)}, f32[1,4,10,2048]{3,2,1,0:T(8,128)}, u32[]{:S(2)}) copy-start(f32[1,4,10,2048]{3,2,1,0:T(8,128)} %get-tuple-element.51) | copy-start | bytes 983044
  44.2 6.8 %copy-start.10 = (f32[9,2048]{1,0:T(8,128)S(1)}, f32[9,2048]{1,0:T(8,128)}, u32[]{:S(2)}) copy-start(f32[9,2048]{1,0:T(8,128)} %broadcast_multiply_fusion.4) | copy-start | bytes 221188
  44.2 6.8 %copy-start.11 = (f32[9,2048]{1,0:T(8,128)S(1)}, f32[9,2048]{1,0:T(8,128)}, u32[]{:S(2)}) copy-start(f32[9,2048]{1,0:T(8,128)} %broadcast_multiply_fusion.5) | copy-start | bytes 221188
  44.2 6.8 %copy-start.13 = (f32[10,2048]{1,0:T(8,128)S(1)}, f32[10,2048]{1,0:T(8,128)}, u32[]{:S(2)}) copy-start(f32[10,2048]{1,0:T(8,128)} %param.16) | copy-start | bytes 245764
  44.3 6.8 %copy-start.15 = (f32[10,2048]{1,0:T(8,128)S(1)}, f32[10,2048]{1,0:T(8,128)}, u32[]{:S(2)}) copy-start(f32[10,2048]{1,0:T(8,128)} %param.17) | copy-start | bytes 245764
  44.3 6.8 %copy-start.17 = (s32[10,2048]{1,0:T(8,128)S(1)}, s32[10,2048]{1,0:T(8,128)}, u32[]{:S(2)}) copy-start(s32[10,2048]{1,0:T(8,128)} %param.18) | copy-start | bytes 245764
  44.3 6.8 %copy-start.21 = (f32[10,2048]{1,0:T(8,128)S(1)}, f32[10,2048]{1,0:T(8,128)}, u32[]{:S(2)}) copy-start(f32[10,2048]{1,0:T(8,128)} %param.15) | copy-start | bytes 245764
  56.2 5.3 %copy-start.18 = (f32[2,10,256]{2,1,0:T(8,128)}, f32[2,10,256]{2,1,0:T(8,128)S(1)}, u32[]{:S(2)}) copy-start(f32[2,10,256]{2,1,0:T(8,128)S(1)} %fusion.59) | copy-start | bytes 61444
  63.4 32.9 %collective-permute-start.6 = (f32[2,4,10,256]{3,2,1,0:T(8,128)}, f32[2,4,10,256]{3,2,1,0:T(8,128)}, u32[]{:S(2)}, u32[]{:S(2)}) collective-permute-start(f32[2,4,10,256]{3,2,1,0:T(8,128)} %get-tuple-element.48), channel_id=1, source_target_pairs={{0,32},{8,40},{16,48},{24,56},{32,0},{40,8},{48,16},{56,24},{64,96... | collective-permute-start | bytes 245768 | tf_op jit(solution)/shard_map/ppermute | solution.py:10
  67.4 30.7 %collective-permute-start.5 = (f32[2,4,10,256]{3,2,1,0:T(8,128)}, f32[2,4,10,256]{3,2,1,0:T(8,128)}, u32[]{:S(2)}, u32[]{:S(2)}) collective-permute-start(f32[2,4,10,256]{3,2,1,0:T(8,128)} %get-tuple-element.49), channel_id=1, source_target_pairs={{0,16},{8,24},{16,0},{24,8},{32,48},{40,56},{48,32},{56,40},{64,80... | collective-permute-start | bytes 245768 | tf_op jit(solution)/shard_map/ppermute | solution.py:10
  70.0 29.9 %collective-permute-start.7 = (f32[2,4,10,256]{3,2,1,0:T(8,128)}, f32[2,4,10,256]{3,2,1,0:T(8,128)}, u32[]{:S(2)}, u32[]{:S(2)}) collective-permute-start(f32[2,4,10,256]{3,2,1,0:T(8,128)} %get-tuple-element.47), channel_id=1, source_target_pairs={{0,64},{8,72},{16,80},{24,88},{32,96},{40,104},{48,112},{56,120},{... | collective-permute-start | bytes 245768 | tf_op jit(solution)/shard_map/ppermute | solution.py:10
  76.7 25.1 %collective-permute-start.4 = (f32[2,4,10,256]{3,2,1,0:T(8,128)}, f32[2,4,10,256]{3,2,1,0:T(8,128)}, u32[]{:S(2)}, u32[]{:S(2)}) collective-permute-start(f32[2,4,10,256]{3,2,1,0:T(8,128)} %get-tuple-element.46), channel_id=1, source_target_pairs={{0,8},{8,0},{16,24},{24,16},{32,40},{40,32},{48,56},{56,48},{64,72... | collective-permute-start | bytes 245768 | tf_op jit(solution)/shard_map/ppermute | solution.py:10
  79.4 7.7 %copy-start.20 = (f32[2,10,256]{2,1,0:T(8,128)S(1)}, f32[2,10,256]{2,1,0:T(8,128)}, u32[]{:S(2)}) copy-start(f32[2,10,256]{2,1,0:T(8,128)} %copy-done.19) | copy-start | bytes 61444
  81.4 8.7 %copy-start.22 = (f32[4,2048]{1,0:T(4,128)S(1)}, f32[4,2048]{1,0:T(4,128)}, u32[]{:S(2)}) copy-start(f32[4,2048]{1,0:T(4,128)} %param.19) | copy-start | bytes 98308
  (9 other events, 24.5 us)
Sparse Core Ops, SparseCore 0:
  79.5 48.0 all-gather.2
